TPU v7x, 128 devices: a whole 4x4x4 slice. The times are simulated.
128 devices in a mesh: gx: 8 (over z, core), gy: 16 (over y, x).
Axes of the slice: x: 4, y: 4, z: 4, core: 2. Of those that a mesh axis runs over, the one named last changes fastest.
Arguments:
- records: bfloat16 [98304, 2048], P(('gx', 'gy')), may hold values from -4000 to 4000
- record_owner: int32 [98304], P(('gx', 'gy')), may hold values from 0 to 127, as said below
- record_field: int32 [98304], P(('gx', 'gy')), may hold values from 0 to 767, as said below
- filter_taps: float32 [2, 9], replicated, may hold values from 0.02 to 0.3
Outputs:
- modes: float32 [256, 3, 262144], P(None, None, ('gx', 'gy'))
- r_factor: float32 [256, 256], replicated
- first_factor: float32 [256, 256], replicated
Inputs may be any that keep to these rules, and one draw needn't show every extreme that they name: `record_owner`: A device sends at most 12 records to any one owner; every device sends exactly 12 records to the owner whose index is its own plus 128 / 2, counted round; every owner is named by exactly 768 records over all devices. `record_field`: over all devices each pair of owner and field number occurs in exactly one record; field number 3 * s + c holds velocity component c of snapshot s.
All inputs are finite; a program needn't handle non-finite values.
Results may differ from a plain program's by a relative error of at most 0.0003.
Values may be sent and summed in bfloat16 or wider, within the bound.
No kernel may reach another device: no remote copies, remote signals or barrier semaphores. Data moves between devices by JAX's collectives and lax.ppermute only.
A program may use at most 128 MiB of HBM per device.

v0:
```python
import math

import jax
import jax.numpy as jnp
from jax import lax
from jax.sharding import PartitionSpec as P

SNAP = 256
PX = 16
PZ = 128


def circulant(tap_row, period):
    places = jnp.arange(period, dtype=jnp.int32)
    offsets = jnp.arange(9, dtype=jnp.int32) - 4
    target = (places[None, :, None] + offsets[:, None, None]) % period
    onehot = (target == places[None, None, :]).astype(jnp.float32)
    return jnp.einsum("k,kxa->xa", tap_row, onehot, precision=lax.Precision.HIGHEST)


def filter_fields(fields, stream_filter, span_filter):
    planes = fields.reshape(fields.shape[0], PX, PZ)
    planes = jnp.einsum("xa,faz->fxz", stream_filter, planes, precision=lax.Precision.HIGHEST)
    planes = jnp.einsum("fxb,zb->fxz", planes, span_filter, precision=lax.Precision.HIGHEST)
    return planes.reshape(fields.shape[0], PX * PZ)


def gram_of(matrix):
    return lax.dot_general(
        matrix,
        matrix,
        (((1,), (1,)), ((), ())),
        precision=lax.Precision.HIGHEST,
        preferred_element_type=jnp.float32,
    )


def sum_over_devices(part, axes, devices_all):
    rows = part.reshape(devices_all, -1)
    rows = lax.all_to_all(rows, axes, 0, 0, tiled=True)
    total = jnp.sum(rows, axis=0, keepdims=True)
    total = jnp.broadcast_to(total, rows.shape)
    total = lax.all_to_all(total, axes, 0, 0, tiled=True)
    return total.reshape(part.shape)


def local(records, record_owner, record_field, filter_taps):
    devices_all = lax.axis_size(("gx", "gy"))
    rec_count = records.shape[0]
    cells = records.shape[1]
    capacity = 2 * (rec_count // devices_all)
    stream_filter = circulant(filter_taps[0], PX)
    span_filter = circulant(filter_taps[1], PZ)
    onehot = (record_owner[:, None] == jnp.arange(devices_all, dtype=jnp.int32)[None, :]).astype(
        jnp.int32
    )
    position = jnp.sum((jnp.cumsum(onehot, axis=0) - 1) * onehot, axis=1)
    slot = record_owner * capacity + position
    places = jnp.arange(devices_all * capacity, dtype=jnp.int32)
    pick = slot[None, :] == places[:, None]
    buffer = jnp.dot(
        pick.astype(jnp.bfloat16), records, preferred_element_type=jnp.float32
    ).astype(jnp.bfloat16)
    labels = jnp.sum(jnp.where(pick, record_field[None, :] + 1, 0), axis=1) - 1
    arrived, arrived_labels = (
        lax.all_to_all(
            buffer.reshape(devices_all, capacity, cells),
            ("gx", "gy"),
            split_axis=0,
            concat_axis=0,
            tiled=True,
        ),
        lax.all_to_all(
            labels.reshape(devices_all, capacity),
            ("gx", "gy"),
            split_axis=0,
            concat_axis=0,
            tiled=True,
        ),
    )
    flat_data = arrived.reshape(devices_all * capacity, cells)
    flat_labels = arrived_labels.reshape(devices_all * capacity)
    order = flat_labels[None, :] == jnp.arange(rec_count, dtype=jnp.int32)[:, None]
    fields = jnp.dot(order.astype(jnp.bfloat16), flat_data, preferred_element_type=jnp.float32)
    fields = filter_fields(fields, stream_filter, span_filter)
    matrix = fields.reshape(SNAP, 3 * cells)
    lower_one = jnp.linalg.cholesky(sum_over_devices(gram_of(matrix), ("gx", "gy"), devices_all))
    basis_one = jax.scipy.linalg.solve_triangular(lower_one, matrix, lower=True)
    lower_two = jnp.linalg.cholesky(sum_over_devices(gram_of(basis_one), ("gx", "gy"), devices_all))
    scale = math.sqrt(3.0 * cells * devices_all)
    modes = jax.scipy.linalg.solve_triangular(lower_two, basis_one, lower=True) * scale
    r_factor = (
        jnp.dot(
            lower_two.T,
            lower_one.T,
            precision=lax.Precision.HIGHEST,
            preferred_element_type=jnp.float32,
        )
        / scale
    )
    first_factor = lower_one.T / scale
    return (modes.reshape(SNAP, 3, cells), r_factor, first_factor)


def solution(mesh):
    placed = (P(("gx", "gy"), None), P(("gx", "gy")), P(("gx", "gy")), P())
    return jax.shard_map(
        local,
        mesh=mesh,
        in_specs=placed,
        out_specs=(P(None, None, ("gx", "gy")), P(), P()),
        check_vma=False,
    )
```

profile of v0, /device:TPU:1, one launch (start us, length us, event | category | flops | bytes accessed | tf_op | source)
XLA Modules:
  0.0 467.3 jit_solution(7321578132998953763)
XLA Ops:
  6.8 11.5 %all-to-all-start = ((s32[128,1,12]{2,1,0:T(1,128)}), s32[128,1,12]{2,1,0:T(1,128)S(1)}, u32[]{:S(2)}, u32[]{:S(2)}) async-start(s32[128,1,12]{2,1,0:T(1,128)} %bitcast.4), calls=%async_computation | async-start | bytes 131072 | tf_op jit(solution)/shard_map/all_to_all | solution.py:73
  18.3 6.9 %convolution_convert_fusion = bf16[1536,2048]{1,0:T(8,128)(2,1)} fusion(bf16[768,2048]{1,0:T(8,128)(2,1)S(1)} %copy-done, s32[768]{0:T(1024)S(1)} %get-tuple-element.67), kind=kOutput, calls=%fused_computation.4 | convolution fusion | flops 4836163584 | bytes 9440256 | tf_op jit(solution)/shard_map/dot_general | solution.py:61
  25.2 10.6 %reshape.186 = bf16[128,12,2048]{2,1,0:T(8,128)(2,1)} reshape(bf16[1536,2048]{1,0:T(8,128)(2,1)} %convolution_convert_fusion) | data formatting | bytes 12582912 | tf_op jit(solution)/shard_map/reshape | solution.py:67
  35.8 10.2 %all-to-all-start.1 = ((bf16[128,12,2048]{2,1,0:T(8,128)(2,1)}), bf16[128,12,2048]{2,1,0:T(8,128)(2,1)}, u32[]{:S(2)}, u32[]{:S(2)}) async-start(bf16[128,12,2048]{2,1,0:T(8,128)(2,1)} %reshape.186), calls=%async_computation.1 | async-start | bytes 16777216 | tf_op jit(solution)/shard_map/all_to_all | solution.py:66
  48.7 96.5 %all-to-all-done.1 = bf16[128,12,2048]{2,1,0:T(8,128)(2,1)} async-done(((bf16[128,12,2048]{2,1,0:T(8,128)(2,1)}), bf16[128,12,2048]{2,1,0:T(8,128)(2,1)}, u32[]{:S(2)}, u32[]{:S(2)}) %all-to-all-start.1) | async-done | bytes 6291488 | tf_op jit(solution)/shard_map/all_to_all | solution.py:66
  145.2 10.7 %reshape.187 = bf16[1536,2048]{1,0:T(8,128)(2,1)} reshape(bf16[128,12,2048]{2,1,0:T(8,128)(2,1)} %all-to-all-done.1) | data formatting | bytes 12582912 | tf_op jit(solution)/shard_map/reshape | solution.py:81
  155.9 8.7 %copy.36 = bf16[2048,1536]{1,0:T(8,128)(2,1)} copy(bf16[2048,1536]{0,1:T(8,128)(2,1)} %bitcast.107) | data formatting | bytes 12582912 | tf_op jit(solution)/shard_map/dot_general | solution.py:84
  164.6 7.4 %fusion.9 = f32[768,16,128]{2,0,1:T(8,128)S(1)} fusion(bf16[16,128,1536]{2,1,0:T(8,128)(2,1)} %bitcast.109, s32[1536]{0:T(1024)S(1)} %eq.91), kind=kOutput, calls=%fused_computation.20 | convolution fusion | flops 4833017856 | bytes 12589056 | tf_op jit(solution)/shard_map/dot_general | solution.py:84
  172.0 9.4 %fusion.6 = f32[768,128,16]{1,2,0:T(8,128)S(1)} fusion(f32[16,16,1]{1,0,2:T(8,128)S(1)} %bitcast.113, f32[768,16,128]{2,0,1:T(8,128)S(1)} %fusion.9), kind=kOutput, calls=%fused_computation.14 | convolution fusion | flops 301989888 | bytes 12583936 | tf_op jit(solution)/shard_map/xa,faz->fxz/dot_general | solution.py:23
  181.4 7.3 %fusion.4 = f32[768,16,128]{2,1,0:T(8,128)} fusion(f32[128,128,1]{1,0,2:T(8,128)S(1)} %bitcast.110, f32[768,128,16]{1,2,0:T(8,128)S(1)} %fusion.6), kind=kOutput, calls=%fused_computation.12 | convolution fusion | flops 2415919104 | bytes 12648448 | tf_op jit(solution)/shard_map/fxb,zb->fxz/dot_general | solution.py:24
  188.7 7.3 %reshape_reshape.3 = f32[256,6144]{1,0:T(8,128)} reshape(f32[768,16,128]{2,1,0:T(8,128)} %fusion.4) | data formatting | bytes 12582912 | tf_op jit(solution)/shard_map/reshape;reshape | solution.py:86
  196.0 17.1 %fusion.63 = f32[256,256]{1,0:T(8,128)S(1)} fusion(f32[256,6144]{1,0:T(8,128)} %reshape_reshape.3), kind=kOutput, calls=%fused_computation.116 | convolution fusion | flops 4831838208 | bytes 6553600 | tf_op jit(solution)/shard_map/dot_general | solution.py:29
  214.1 12.1 %all-to-all-start.2 = ((f32[128,1,512]{2,1,0:T(1,128)}), f32[128,1,512]{2,1,0:T(1,128)S(1)}, u32[]{:S(2)}, u32[]{:S(2)}) async-start(f32[128,1,512]{2,1,0:T(1,128)} %all_to_all.35), calls=%async_computation.2 | async-start | bytes 524288 | tf_op jit(solution)/shard_map/all_to_all | solution.py:40
  226.2 11.3 %all-to-all-done.2 = f32[128,1,512]{2,1,0:T(1,128)S(1)} async-done(((f32[128,1,512]{2,1,0:T(1,128)}), f32[128,1,512]{2,1,0:T(1,128)S(1)}, u32[]{:S(2)}, u32[]{:S(2)}) %all-to-all-start.2) | async-done | bytes 262176 | tf_op jit(solution)/shard_map/all_to_all | solution.py:40
  238.5 4.5 all-to-all-start.3
  243.0 11.2 %all-to-all-done.3 = f32[128,1,512]{2,1,0:T(1,128)S(1)} async-done(((f32[128,1,512]{2,1,0:T(1,128)}), f32[128,1,512]{2,1,0:T(1,128)S(1)}, u32[]{:S(2)}, u32[]{:S(2)}) %all-to-all-start.3) | async-done | bytes 262176 | tf_op jit(solution)/shard_map/all_to_all | solution.py:43
  255.0 11.7 %cholesky.130 = f32[128,128]{1,0:T(8,128)S(1)} custom-call(f32[128,128]{1,0:T(8,128)S(1)} %cholesky.194), custom_call_target="Cholesky" | custom-call | tf_op jit(solution)/shard_map/jit(cholesky)/cholesky | solution.py:87
  266.8 9.8 %custom-call.13 = f32[1,128,128]{1,2,0:T(8,128)S(1)} custom-call(f32[1,128,128]{2,1,0:T(8,128)S(1)} %get-tuple-element.62), custom_call_target="InvertDiagBlocksLowerTriangular" | custom-call | tf_op jit(solution)/shard_map/jit(cholesky)/cholesky | solution.py:87
  277.1 11.7 %cholesky.147 = f32[128,128]{1,0:T(8,128)S(1)} custom-call(f32[128,128]{1,0:T(8,128)S(1)} %convolution_subtract_fusion.3), custom_call_target="Cholesky" | custom-call | tf_op jit(solution)/shard_map/jit(cholesky)/cholesky | solution.py:87
  292.3 4.0 while.4
  292.9 1.4 bitcast_dynamic-update-slice_fusion.4
  294.9 1.4 bitcast_dynamic-update-slice_fusion.4
  296.3 20.1 %custom-call.14 = f32[2,128,128]{1,2,0:T(8,128)S(1)} custom-call(f32[2,128,128]{2,1,0:T(8,128)S(1)} %get-tuple-element.19), custom_call_target="InvertDiagBlocksLowerTriangular" | custom-call | tf_op jit(solution)/shard_map/jit(_solve_triangular)/triangular_solve | solution.py:88
  316.4 4.8 %fusion.11 = f32[128,6144]{1,0:T(8,128)S(1)} fusion(f32[256,6144]{1,0:T(8,128)} %reshape_reshape.3, f32[2,128,128]{1,2,0:T(8,128)S(1)} %custom-call.14), kind=kOutput, calls=%fused_computation.21 | convolution fusion | flops 1207959552 | bytes 6356992 | tf_op jit(solution)/shard_map/jit(_solve_triangular)/triangular_solve | solution.py:88
  321.2 2.9 convolution_subtract_fusion.1
  324.2 2.9 fusion.41
  327.1 1.7 copy-done.3
  328.7 6.1 %fusion = f32[256,256]{1,0:T(8,128)} fusion(f32[128,6144]{1,0:T(8,128)S(1)} %fusion.41, f32[128,6144]{1,0:T(8,128)S(1)} %fusion.11), kind=kOutput, calls=%fused_computation.7 | convolution fusion | flops 4833411072 | bytes 6553600 | tf_op jit(solution)/shard_map/dot_general | solution.py:29
  334.8 1.2 all_to_all.36
  336.0 15.6 %all_to_all.43 = f32[128,1,512]{2,1,0:T(1,128)} all-to-all(f32[128,1,512]{2,1,0:T(1,128)S(1)} %all_to_all.36), channel_id=1, replica_groups=mesh['gx'=8,'gy'=16] {'gx','gy'}, dimensions={0} | all-to-all | bytes 524288 | tf_op jit(solution)/shard_map/all_to_all | solution.py:40
  353.6 4.2 all-to-all-start.5
  357.8 1.8 copy.46
  359.6 9.5 %all-to-all-done.5 = f32[128,1,512]{2,1,0:T(1,128)S(1)} async-done(((f32[128,1,512]{2,1,0:T(1,128)}), f32[128,1,512]{2,1,0:T(1,128)S(1)}, u32[]{:S(2)}, u32[]{:S(2)}) %all-to-all-start.5) | async-done | bytes 262176 | tf_op jit(solution)/shard_map/all_to_all | solution.py:43
  369.1 1.3 reduce.12
  374.0 11.7 %cholesky.164 = f32[128,128]{1,0:T(8,128)S(1)} custom-call(f32[128,128]{1,0:T(8,128)S(1)} %cholesky.197), custom_call_target="Cholesky" | custom-call | tf_op jit(solution)/shard_map/jit(cholesky)/cholesky | solution.py:89
  385.8 9.8 %custom-call.15 = f32[1,128,128]{1,2,0:T(8,128)S(1)} custom-call(f32[1,128,128]{2,1,0:T(8,128)S(1)} %get-tuple-element.58), custom_call_target="InvertDiagBlocksLowerTriangular" | custom-call | tf_op jit(solution)/shard_map/jit(cholesky)/cholesky | solution.py:89
  397.7 11.7 %cholesky.181 = f32[128,128]{1,0:T(8,128)S(1)} custom-call(f32[128,128]{1,0:T(8,128)S(1)} %convolution_subtract_fusion.2), custom_call_target="Cholesky" | custom-call | tf_op jit(solution)/shard_map/jit(cholesky)/cholesky | solution.py:89
  412.2 2.2 convolution_multiply_fusion
  415.1 5.8 %while.5 = (s32[]{:T(128)}, f32[256,256]{1,0:T(8,128)}, s32[2,2]{1,0:T(2,128)S(1)}, f32[2,128,128]{2,1,0:T(8,128)S(1)}, s32[]{:T(128)}) while((s32[]{:T(128)}, f32[256,256]{1,0:T(8,128)}, s32[2,2]{1,0:T(2,128)S(1)}, f32[2,128,128]{2,1,0:T(8,128)S(1)}, s32[]{:T(128)}) %tuple.58), condition=%wide.while_cond.clone, body=%wide.while_body.clone.sunk | while | flops 2 | bytes 131181 | solution.py:91
  415.8 2.3 bitcast_dynamic-update-slice_fusion.5
  418.7 2.2 bitcast_dynamic-update-slice_fusion.5
  420.9 19.9 %custom-call.16 = f32[2,128,128]{1,2,0:T(8,128)S(1)} custom-call(f32[2,128,128]{2,1,0:T(8,128)S(1)} %get-tuple-element.20), custom_call_target="InvertDiagBlocksLowerTriangular" | custom-call | tf_op jit(solution)/shard_map/jit(_solve_triangular)/triangular_solve | solution.py:91
  440.8 2.8 fusion.37
  443.7 3.8 convolution_subtract_fusion
  447.4 2.8 fusion.36
  450.3 3.2 maximum_multiply_fusion
  453.5 6.6 %copy.44 = f32[256,6144]{0,1:T(8,128)} copy(f32[256,6144]{1,0:T(8,128)} %maximum_multiply_fusion) | data formatting | bytes 12582912 | tf_op jit(solution)/shard_map/mul | solution.py:91
  460.1 6.8 %copy.45 = f32[256,3,2048]{2,0,1:T(8,128)} copy(f32[256,3,2048]{0,2,1:T(8,128)} %bitcast.108) | data formatting | bytes 12582912
  (81 shorter events, 26.6 us)
Async XLA Ops:
  0.6 17.7 %copy-start = (bf16[768,2048]{1,0:T(8,128)(2,1)S(1)}, bf16[768,2048]{1,0:T(8,128)(2,1)}, u32[]{:S(2)}) copy-start(bf16[768,2048]{1,0:T(8,128)(2,1)} %param.7) | copy-start | bytes 9437188
  1.8 0.8 copy-start.6
  6.8 29.0 %all-to-all-start = ((s32[128,1,12]{2,1,0:T(1,128)}), s32[128,1,12]{2,1,0:T(1,128)S(1)}, u32[]{:S(2)}, u32[]{:S(2)}) async-start(s32[128,1,12]{2,1,0:T(1,128)} %bitcast.4), calls=%async_computation | async-start | bytes 131072 | tf_op jit(solution)/shard_map/all_to_all | solution.py:73
  35.8 10.5 %copy-start.8 = (f32[2,9]{1,0:T(2,128)S(1)}, f32[2,9]{1,0:T(2,128)}, u32[]{:S(2)}) copy-start(f32[2,9]{1,0:T(2,128)} %param.10) | copy-start | bytes 220
  35.8 109.4 %all-to-all-start.1 = ((bf16[128,12,2048]{2,1,0:T(8,128)(2,1)}), bf16[128,12,2048]{2,1,0:T(8,128)(2,1)}, u32[]{:S(2)}, u32[]{:S(2)}) async-start(bf16[128,12,2048]{2,1,0:T(8,128)(2,1)} %reshape.186), calls=%async_computation.1 | async-start | bytes 16777216 | tf_op jit(solution)/shard_map/all_to_all | solution.py:66
  214.1 23.4 %all-to-all-start.2 = ((f32[128,1,512]{2,1,0:T(1,128)}), f32[128,1,512]{2,1,0:T(1,128)S(1)}, u32[]{:S(2)}, u32[]{:S(2)}) async-start(f32[128,1,512]{2,1,0:T(1,128)} %all_to_all.35), calls=%async_computation.2 | async-start | bytes 524288 | tf_op jit(solution)/shard_map/all_to_all | solution.py:40
  238.5 15.7 %all-to-all-start.3 = ((f32[128,1,512]{2,1,0:T(1,128)}), f32[128,1,512]{2,1,0:T(1,128)S(1)}, u32[]{:S(2)}, u32[]{:S(2)}) async-start(f32[128,1,512]{2,1,0:T(1,128)} %broadcast_in_dim.14), calls=%async_computation.3 | async-start | bytes 524288 | tf_op jit(solution)/shard_map/all_to_all | solution.py:43
  288.9 7.4 %copy-start.5 = (f32[256,256]{1,0:T(8,128)}, f32[256,256]{1,0:T(8,128)S(1)}, u32[]{:S(2)}) copy-start(f32[256,256]{1,0:T(8,128)S(1)} %get-tuple-element.60) | copy-start | bytes 786436
  316.4 4.9 %copy-start.2 = (f32[256,6144]{1,0:T(8,128)S(1)}, f32[256,6144]{1,0:T(8,128)}, u32[]{:S(2)}) copy-start(f32[256,6144]{1,0:T(8,128)} %reshape_reshape.3) | copy-start | bytes 18874372
  327.1 1.7 copy-start.3
  353.6 15.5 %all-to-all-start.5 = ((f32[128,1,512]{2,1,0:T(1,128)}), f32[128,1,512]{2,1,0:T(1,128)S(1)}, u32[]{:S(2)}, u32[]{:S(2)}) async-start(f32[128,1,512]{2,1,0:T(1,128)} %broadcast_in_dim.19), calls=%async_computation.5 | async-start | bytes 524288 | tf_op jit(solution)/shard_map/all_to_all | solution.py:43
  373.3 0.7 copy-start.7
  440.8 2.9 copy-start.4
  460.1 6.8 %copy-start.1 = (bf16[768,2048]{1,0:T(8,128)(2,1)S(1)}, bf16[768,2048]{1,0:T(8,128)(2,1)}, u32[]{:S(2)}) copy-start(bf16[768,2048]{1,0:T(8,128)(2,1)} %param.7) | copy-start | bytes 9437188
where the time goes:
time: 476 us; the launch traced here: 467 us
  waiting for transfers between devices  128 us (27%)
  other arithmetic  123 us (26%)
  matrix products  79.8 us (17%)
  local copies, waits for them, and re-layouts  73.7 us (15%)
  starting transfers between devices  42.5 us (9%)
  blocking collectives  15.6 us (3%)
    all_to_all x1, waiting for transfers between devices, local(): lax.all_to_all(buffer.reshape(devices_all, capacity, cells), ('gx', 'gy')...  96.5 us
    another operation x7, other arithmetic, local(): jnp.linalg.cholesky(sum_over_devices(gram_of(basis_one), ('gx', 'gy'), de...  34.7 us
    another operation x7, other arithmetic, local(): jnp.linalg.cholesky(sum_over_devices(gram_of(matrix), ('gx', 'gy'), devic...  34.6 us
    dot_general x2, matrix products, gram_of(): lax.dot_general(matrix, matrix, (((1,), (1,)), ((), ())), precision=lax.P...  23.2 us
    all_to_all x2, waiting for transfers between devices, sum_over_devices(): total = lax.all_to_all(total, axes, 0, 0, tiled=True)  20.7 us
    another operation x2, other arithmetic, local(): jax.scipy.linalg.solve_triangular(lower_two, basis_one, lower=True) * scale  20.6 us
    another operation x2, other arithmetic, local(): basis_one = jax.scipy.linalg.solve_triangular(lower_one, matrix, lower=True)  20.1 us
    all_to_all x1, blocking collectives, sum_over_devices(): rows = lax.all_to_all(rows, axes, 0, 0, tiled=True)  15.6 us
  transfers between devices with their start and end apart: 5, of which 4 were waited for; matrix products, arithmetic and copies ran while one was open for 5% of the time, Pallas kernels for 0%

commit v1 on v0

--- a/solution.py
+++ b/solution.py
@@ -48,7 +48,7 @@
     devices_all = lax.axis_size(("gx", "gy"))
     rec_count = records.shape[0]
     cells = records.shape[1]
-    capacity = 2 * (rec_count // devices_all)
+    capacity = -(-2 * (rec_count // devices_all) // 16) * 16
     stream_filter = circulant(filter_taps[0], PX)
     span_filter = circulant(filter_taps[1], PZ)
     onehot = (record_owner[:, None] == jnp.arange(devices_all, dtype=jnp.int32)[None, :]).astype(

time: 476 us -> 463 us (0.973)
  local copies, waits for them, and re-layouts: 73.7 us -> 56 us
    reshape x1 -> x0, local copies, waits for them, and re-layouts: 10.6 us -> none  [local(): buffer.reshape(devices_all, capacity, cells)]
    dot_general x1 -> x0, local copies, waits for them, and re-layouts: 8.67 us -> none  [local(): jnp.dot(order.astype(jnp.bfloat16), flat_data, preferred_element_type=jnp...]
  transfers between devices with their start and end apart: 5 -> 5, of which waited for: 4 -> 5; matrix products, arithmetic and copies ran while one was open for 5% -> 3% of each run, Pallas kernels for 0% -> 0%
where the time goes in v1:
time: 463 us; the launch traced here: 454 us
  waiting for transfers between devices  129 us (28%)
  other arithmetic  123 us (27%)
  matrix products  83.6 us (18%)
  local copies, waits for them, and re-layouts  56 us (12%)
  starting transfers between devices  41.8 us (9%)
  blocking collectives  15.6 us (3%)
    all_to_all x1, waiting for transfers between devices, local(): lax.all_to_all(buffer.reshape(devices_all, capacity, cells), ('gx', 'gy')...  96.6 us
    another operation x7, other arithmetic, local(): jnp.linalg.cholesky(sum_over_devices(gram_of(basis_one), ('gx', 'gy'), de...  34.7 us
    another operation x7, other arithmetic, local(): jnp.linalg.cholesky(sum_over_devices(gram_of(matrix), ('gx', 'gy'), devic...  34.6 us
    dot_general x2, matrix products, gram_of(): lax.dot_general(matrix, matrix, (((1,), (1,)), ((), ())), precision=lax.P...  23.2 us
    all_to_all x2, waiting for transfers between devices, sum_over_devices(): total = lax.all_to_all(total, axes, 0, 0, tiled=True)  20.7 us
    another operation x2, other arithmetic, local(): jax.scipy.linalg.solve_triangular(lower_two, basis_one, lower=True) * scale  20.6 us
    another operation x2, other arithmetic, local(): basis_one = jax.scipy.linalg.solve_triangular(lower_one, matrix, lower=True)  20.1 us
    all_to_all x1, blocking collectives, sum_over_devices(): rows = lax.all_to_all(rows, axes, 0, 0, tiled=True)  15.6 us
  transfers between devices with their start and end apart: 5, of which 5 were waited for; matrix products, arithmetic and copies ran while one was open for 3% of the time, Pallas kernels for 0%

profile of v1, /device:TPU:1, one launch (start us, length us, event | category | flops | bytes accessed | tf_op | source)
XLA Modules:
  0.0 453.7 jit_solution(16219094705699375142)
XLA Ops:
  6.9 11.5 %all-to-all-start = ((s32[128,1,16]{2,1,0:T(1,128)}), s32[128,1,16]{2,1,0:T(1,128)S(1)}, u32[]{:S(2)}, u32[]{:S(2)}) async-start(s32[128,1,16]{2,1,0:T(1,128)} %bitcast.4), calls=%async_computation | async-start | bytes 131072 | tf_op jit(solution)/shard_map/all_to_all | solution.py:73
  18.5 8.8 %convolution_convert_fusion = bf16[2048,2048]{1,0:T(8,128)(2,1)} fusion(bf16[768,2048]{1,0:T(8,128)(2,1)S(1)} %copy-done, s32[768]{0:T(1024)S(1)} %get-tuple-element.67), kind=kOutput, calls=%fused_computation.4 | convolution fusion | flops 6448218112 | bytes 11537408 | tf_op jit(solution)/shard_map/dot_general | solution.py:61
  28.0 9.5 %all-to-all-start.1 = ((bf16[128,16,2048]{2,1,0:T(8,128)(2,1)}), bf16[128,16,2048]{2,1,0:T(8,128)(2,1)}, u32[]{:S(2)}, u32[]{:S(2)}) async-start(bf16[128,16,2048]{2,1,0:T(8,128)(2,1)} %bitcast.111), calls=%async_computation.1 | async-start | bytes 16777216 | tf_op jit(solution)/shard_map/all_to_all | solution.py:66
  40.1 96.6 %all-to-all-done.1 = bf16[128,16,2048]{2,1,0:T(8,128)(2,1)} async-done(((bf16[128,16,2048]{2,1,0:T(8,128)(2,1)}), bf16[128,16,2048]{2,1,0:T(8,128)(2,1)}, u32[]{:S(2)}, u32[]{:S(2)}) %all-to-all-start.1) | async-done | bytes 8388640 | tf_op jit(solution)/shard_map/all_to_all | solution.py:66
  136.7 12.3 %copy.36 = bf16[2048,2048]{0,1:T(8,128)(2,1)} copy(bf16[2048,2048]{1,0:T(8,128)(2,1)} %bitcast.7) | data formatting | bytes 16777216 | tf_op jit(solution)/shard_map/reshape | solution.py:81
  149.0 9.3 %fusion.9 = f32[768,16,128]{2,0,1:T(8,128)S(1)} fusion(bf16[16,128,2048]{2,1,0:T(8,128)(2,1)} %bitcast.112, s32[2048]{0:T(1024)S(1)} %eq.91), kind=kOutput, calls=%fused_computation.20 | convolution fusion | flops 6444023808 | bytes 14688256 | tf_op jit(solution)/shard_map/dot_general | solution.py:84
  158.3 9.4 %fusion.6 = f32[768,128,16]{1,2,0:T(8,128)S(1)} fusion(f32[16,16,1]{1,0,2:T(8,128)S(1)} %bitcast.116, f32[768,16,128]{2,0,1:T(8,128)S(1)} %fusion.9), kind=kOutput, calls=%fused_computation.14 | convolution fusion | flops 301989888 | bytes 12583936 | tf_op jit(solution)/shard_map/xa,faz->fxz/dot_general | solution.py:23
  167.7 7.3 %fusion.4 = f32[768,16,128]{2,1,0:T(8,128)} fusion(f32[128,128,1]{1,0,2:T(8,128)S(1)} %bitcast.113, f32[768,128,16]{1,2,0:T(8,128)S(1)} %fusion.6), kind=kOutput, calls=%fused_computation.12 | convolution fusion | flops 2415919104 | bytes 12648448 | tf_op jit(solution)/shard_map/fxb,zb->fxz/dot_general | solution.py:24
  175.0 7.3 %reshape_reshape.3 = f32[256,6144]{1,0:T(8,128)} reshape(f32[768,16,128]{2,1,0:T(8,128)} %fusion.4) | data formatting | bytes 12582912 | tf_op jit(solution)/shard_map/reshape;reshape | solution.py:86
  182.4 17.1 %fusion.63 = f32[256,256]{1,0:T(8,128)S(1)} fusion(f32[256,6144]{1,0:T(8,128)} %reshape_reshape.3), kind=kOutput, calls=%fused_computation.116 | convolution fusion | flops 4831838208 | bytes 6553600 | tf_op jit(solution)/shard_map/dot_general | solution.py:29
  200.5 12.1 %all-to-all-start.2 = ((f32[128,1,512]{2,1,0:T(1,128)}), f32[128,1,512]{2,1,0:T(1,128)S(1)}, u32[]{:S(2)}, u32[]{:S(2)}) async-start(f32[128,1,512]{2,1,0:T(1,128)} %all_to_all.35), calls=%async_computation.2 | async-start | bytes 524288 | tf_op jit(solution)/shard_map/all_to_all | solution.py:40
  212.6 11.3 %all-to-all-done.2 = f32[128,1,512]{2,1,0:T(1,128)S(1)} async-done(((f32[128,1,512]{2,1,0:T(1,128)}), f32[128,1,512]{2,1,0:T(1,128)S(1)}, u32[]{:S(2)}, u32[]{:S(2)}) %all-to-all-start.2) | async-done | bytes 262176 | tf_op jit(solution)/shard_map/all_to_all | solution.py:40
  224.9 4.5 all-to-all-start.3
  229.4 11.2 %all-to-all-done.3 = f32[128,1,512]{2,1,0:T(1,128)S(1)} async-done(((f32[128,1,512]{2,1,0:T(1,128)}), f32[128,1,512]{2,1,0:T(1,128)S(1)}, u32[]{:S(2)}, u32[]{:S(2)}) %all-to-all-start.3) | async-done | bytes 262176 | tf_op jit(solution)/shard_map/all_to_all | solution.py:43
  241.4 11.7 %cholesky.130 = f32[128,128]{1,0:T(8,128)S(1)} custom-call(f32[128,128]{1,0:T(8,128)S(1)} %cholesky.194), custom_call_target="Cholesky" | custom-call | tf_op jit(solution)/shard_map/jit(cholesky)/cholesky | solution.py:87
  253.2 9.8 %custom-call.13 = f32[1,128,128]{1,2,0:T(8,128)S(1)} custom-call(f32[1,128,128]{2,1,0:T(8,128)S(1)} %get-tuple-element.62), custom_call_target="InvertDiagBlocksLowerTriangular" | custom-call | tf_op jit(solution)/shard_map/jit(cholesky)/cholesky | solution.py:87
  263.5 11.7 %cholesky.147 = f32[128,128]{1,0:T(8,128)S(1)} custom-call(f32[128,128]{1,0:T(8,128)S(1)} %convolution_subtract_fusion.3), custom_call_target="Cholesky" | custom-call | tf_op jit(solution)/shard_map/jit(cholesky)/cholesky | solution.py:87
  278.6 4.0 while.4
  279.3 1.4 bitcast_dynamic-update-slice_fusion.4
  281.2 1.4 bitcast_dynamic-update-slice_fusion.4
  282.6 20.1 %custom-call.14 = f32[2,128,128]{1,2,0:T(8,128)S(1)} custom-call(f32[2,128,128]{2,1,0:T(8,128)S(1)} %get-tuple-element.19), custom_call_target="InvertDiagBlocksLowerTriangular" | custom-call | tf_op jit(solution)/shard_map/jit(_solve_triangular)/triangular_solve | solution.py:88
  302.7 4.8 %fusion.11 = f32[128,6144]{1,0:T(8,128)S(1)} fusion(f32[256,6144]{1,0:T(8,128)} %reshape_reshape.3, f32[2,128,128]{1,2,0:T(8,128)S(1)} %custom-call.14), kind=kOutput, calls=%fused_computation.21 | convolution fusion | flops 1207959552 | bytes 6356992 | tf_op jit(solution)/shard_map/jit(_solve_triangular)/triangular_solve | solution.py:88
  307.6 2.9 convolution_subtract_fusion.1
  310.6 2.9 fusion.41
  313.4 1.7 copy-done.3
  315.1 6.1 %fusion = f32[256,256]{1,0:T(8,128)} fusion(f32[128,6144]{1,0:T(8,128)S(1)} %fusion.41, f32[128,6144]{1,0:T(8,128)S(1)} %fusion.11), kind=kOutput, calls=%fused_computation.7 | convolution fusion | flops 4833411072 | bytes 6553600 | tf_op jit(solution)/shard_map/dot_general | solution.py:29
  321.2 1.2 all_to_all.36
  322.4 15.6 %all_to_all.43 = f32[128,1,512]{2,1,0:T(1,128)} all-to-all(f32[128,1,512]{2,1,0:T(1,128)S(1)} %all_to_all.36), channel_id=1, replica_groups=mesh['gx'=8,'gy'=16] {'gx','gy'}, dimensions={0} | all-to-all | bytes 524288 | tf_op jit(solution)/shard_map/all_to_all | solution.py:40
  338.0 1.2 reduce_sum.39
  340.0 4.2 all-to-all-start.5
  344.2 1.8 copy.46
  346.0 9.5 %all-to-all-done.5 = f32[128,1,512]{2,1,0:T(1,128)S(1)} async-done(((f32[128,1,512]{2,1,0:T(1,128)}), f32[128,1,512]{2,1,0:T(1,128)S(1)}, u32[]{:S(2)}, u32[]{:S(2)}) %all-to-all-start.5) | async-done | bytes 262176 | tf_op jit(solution)/shard_map/all_to_all | solution.py:43
  355.5 1.3 reduce.12
  360.4 11.7 %cholesky.164 = f32[128,128]{1,0:T(8,128)S(1)} custom-call(f32[128,128]{1,0:T(8,128)S(1)} %cholesky.197), custom_call_target="Cholesky" | custom-call | tf_op jit(solution)/shard_map/jit(cholesky)/cholesky | solution.py:89
  372.1 9.8 %custom-call.15 = f32[1,128,128]{1,2,0:T(8,128)S(1)} custom-call(f32[1,128,128]{2,1,0:T(8,128)S(1)} %get-tuple-element.58), custom_call_target="InvertDiagBlocksLowerTriangular" | custom-call | tf_op jit(solution)/shard_map/jit(cholesky)/cholesky | solution.py:89
  383.0 1.1 convolution_subtract_fusion.2
  384.1 11.7 %cholesky.181 = f32[128,128]{1,0:T(8,128)S(1)} custom-call(f32[128,128]{1,0:T(8,128)S(1)} %convolution_subtract_fusion.2), custom_call_target="Cholesky" | custom-call | tf_op jit(solution)/shard_map/jit(cholesky)/cholesky | solution.py:89
  398.6 2.2 convolution_multiply_fusion
  401.5 5.8 %while.5 = (s32[]{:T(128)}, f32[256,256]{1,0:T(8,128)}, s32[2,2]{1,0:T(2,128)S(1)}, f32[2,128,128]{2,1,0:T(8,128)S(1)}, s32[]{:T(128)}) while((s32[]{:T(128)}, f32[256,256]{1,0:T(8,128)}, s32[2,2]{1,0:T(2,128)S(1)}, f32[2,128,128]{2,1,0:T(8,128)S(1)}, s32[]{:T(128)}) %tuple.58), condition=%wide.while_cond.clone, body=%wide.while_body.clone.sunk | while | flops 2 | bytes 131181 | solution.py:91
  402.1 2.3 bitcast_dynamic-update-slice_fusion.5
  405.1 2.2 bitcast_dynamic-update-slice_fusion.5
  407.3 19.9 %custom-call.16 = f32[2,128,128]{1,2,0:T(8,128)S(1)} custom-call(f32[2,128,128]{2,1,0:T(8,128)S(1)} %get-tuple-element.20), custom_call_target="InvertDiagBlocksLowerTriangular" | custom-call | tf_op jit(solution)/shard_map/jit(_solve_triangular)/triangular_solve | solution.py:91
  427.2 2.8 fusion.37
  430.0 3.8 convolution_subtract_fusion
  433.8 2.8 fusion.36
  436.7 3.2 maximum_multiply_fusion
  439.9 6.6 %copy.44 = f32[256,6144]{0,1:T(8,128)} copy(f32[256,6144]{1,0:T(8,128)} %maximum_multiply_fusion) | data formatting | bytes 12582912 | tf_op jit(solution)/shard_map/mul | solution.py:91
  446.5 6.8 %copy.45 = f32[256,3,2048]{2,0,1:T(8,128)} copy(f32[256,3,2048]{0,2,1:T(8,128)} %bitcast.110) | data formatting | bytes 12582912
  (79 shorter events, 25.1 us)
Async XLA Ops:
  0.6 17.8 %copy-start = (bf16[768,2048]{1,0:T(8,128)(2,1)S(1)}, bf16[768,2048]{1,0:T(8,128)(2,1)}, u32[]{:S(2)}) copy-start(bf16[768,2048]{1,0:T(8,128)(2,1)} %param.7) | copy-start | bytes 9437188
  1.8 0.8 copy-start.6
  6.9 21.0 %all-to-all-start = ((s32[128,1,16]{2,1,0:T(1,128)}), s32[128,1,16]{2,1,0:T(1,128)S(1)}, u32[]{:S(2)}, u32[]{:S(2)}) async-start(s32[128,1,16]{2,1,0:T(1,128)} %bitcast.4), calls=%async_computation | async-start | bytes 131072 | tf_op jit(solution)/shard_map/all_to_all | solution.py:73
  28.0 9.8 %copy-start.8 = (f32[2,9]{1,0:T(2,128)S(1)}, f32[2,9]{1,0:T(2,128)}, u32[]{:S(2)}) copy-start(f32[2,9]{1,0:T(2,128)} %param.10) | copy-start | bytes 220
  28.0 108.7 %all-to-all-start.1 = ((bf16[128,16,2048]{2,1,0:T(8,128)(2,1)}), bf16[128,16,2048]{2,1,0:T(8,128)(2,1)}, u32[]{:S(2)}, u32[]{:S(2)}) async-start(bf16[128,16,2048]{2,1,0:T(8,128)(2,1)} %bitcast.111), calls=%async_computation.1 | async-start | bytes 16777216 | tf_op jit(solution)/shard_map/all_to_all | solution.py:66
  200.5 23.4 %all-to-all-start.2 = ((f32[128,1,512]{2,1,0:T(1,128)}), f32[128,1,512]{2,1,0:T(1,128)S(1)}, u32[]{:S(2)}, u32[]{:S(2)}) async-start(f32[128,1,512]{2,1,0:T(1,128)} %all_to_all.35), calls=%async_computation.2 | async-start | bytes 524288 | tf_op jit(solution)/shard_map/all_to_all | solution.py:40
  224.9 15.7 %all-to-all-start.3 = ((f32[128,1,512]{2,1,0:T(1,128)}), f32[128,1,512]{2,1,0:T(1,128)S(1)}, u32[]{:S(2)}, u32[]{:S(2)}) async-start(f32[128,1,512]{2,1,0:T(1,128)} %broadcast_in_dim.14), calls=%async_computation.3 | async-start | bytes 524288 | tf_op jit(solution)/shard_map/all_to_all | solution.py:43
  275.2 7.4 %copy-start.5 = (f32[256,256]{1,0:T(8,128)}, f32[256,256]{1,0:T(8,128)S(1)}, u32[]{:S(2)}) copy-start(f32[256,256]{1,0:T(8,128)S(1)} %get-tuple-element.60) | copy-start | bytes 786436
  302.7 4.9 %copy-start.2 = (f32[256,6144]{1,0:T(8,128)S(1)}, f32[256,6144]{1,0:T(8,128)}, u32[]{:S(2)}) copy-start(f32[256,6144]{1,0:T(8,128)} %reshape_reshape.3) | copy-start | bytes 18874372
  313.4 1.7 copy-start.3
  340.0 15.5 %all-to-all-start.5 = ((f32[128,1,512]{2,1,0:T(1,128)}), f32[128,1,512]{2,1,0:T(1,128)S(1)}, u32[]{:S(2)}, u32[]{:S(2)}) async-start(f32[128,1,512]{2,1,0:T(1,128)} %broadcast_in_dim.19), calls=%async_computation.5 | async-start | bytes 524288 | tf_op jit(solution)/shard_map/all_to_all | solution.py:43
  359.7 0.7 copy-start.7
  427.2 2.9 copy-start.4
  446.5 6.8 %copy-start.1 = (bf16[768,2048]{1,0:T(8,128)(2,1)S(1)}, bf16[768,2048]{1,0:T(8,128)(2,1)}, u32[]{:S(2)}) copy-start(bf16[768,2048]{1,0:T(8,128)(2,1)} %param.7) | copy-start | bytes 9437188
